TPU v7x, 512 devices: a whole 4x8x8 slice. The times are simulated.
512 devices in a mesh: rx: 8 (over y), tm: 16 (over z, core), bin: 4 (over x).
Axes of the slice: x: 4, y: 8, z: 8, core: 2. Of those that a mesh axis runs over, the one named last changes fastest.
Arguments:
- samples: bfloat16 [4, 4096, 4096], P('bin', 'tm', 'rx'), may hold values from -45 to 45, as said below
- test_matrix: bfloat16 [4, 4096, 512], P('bin', 'tm'), may hold values from -0.09375 to 0.09375
- forgetting: float32 [4, 16, 512], P('bin', 'tm'), may hold values from 0 to 1, as said below
- prior_sketch: bfloat16 [4, 4096, 512], P('bin', 'rx'), may hold values from -6 to 6
Outputs:
- basis: bfloat16 [4, 16, 4096, 512], P('bin', 'tm', 'rx')
- coefficients: float32 [4, 4096, 512], P('bin', 'tm')
Inputs may be any that keep to these rules, and one draw needn't show every extreme that they name: `samples`: real-valued data. `forgetting`: positive factors.
All inputs are finite; a program needn't handle non-finite values.
Results may differ from a plain program's by a relative error of at most 0.015.
Values may be sent and summed in bfloat16 or wider, within the bound.
No kernel may reach another device: no remote copies, remote signals or barrier semaphores. Data moves between devices by JAX's collectives and lax.ppermute only.
A program may use at most 64 MiB of HBM per device.

v0:
```python
import math
import jax
import jax.numpy as jnp
from jax import lax
from jax.sharding import PartitionSpec as P


def prefix_2(part, axis, combine, identity):
    place = lax.axis_index(axis)
    gathered = jax.tree.map(lambda a: lax.all_gather(a, axis), part)
    state = jax.tree.map(lambda a, e: jnp.zeros_like(a) + jnp.asarray(e, a.dtype), part, identity)

    def one(hop, state):
        return combine(
            state, jax.tree.map(lambda a: lax.dynamic_index_in_dim(a, hop, 0, False), gathered)
        )

    return lax.fori_loop(0, place, one, state)


def with_halo(block, sides, width):
    for axis, dim in sides:
        count = lax.axis_size(axis)
        forward = [(i, i + 1) for i in range(count - 1)]
        backward = [(target, source) for source, target in forward]
        low = lax.ppermute(
            lax.slice_in_dim(block, block.shape[dim] - width, None, axis=dim), axis, forward
        )
        high = lax.ppermute(lax.slice_in_dim(block, 0, width, axis=dim), axis, backward)
        block = jnp.concatenate([low, block, high], axis=dim)
    return block


def combine(earlier, later):
    return (earlier[0] * later[0], later[0][None, :] * earlier[1] + later[1])


def sketch_of(block_data, block_test):
    return lax.dot_general(
        block_data, block_test, (((0,), (0,)), ((), ())), preferred_element_type=jnp.float32
    )


def body(samples, test_matrix, forgetting, prior_sketch):
    block_data = samples[0]
    block_test = test_matrix[0]
    own_decay = forgetting[0, 0]
    prior_rows = prior_sketch[0].astype(jnp.float32)
    width = block_test.shape[1]
    rows = block_data.shape[1]
    sketch = sketch_of(block_data, block_test)
    identity = (jnp.ones((width,), jnp.float32), jnp.zeros((rows, width), jnp.float32))
    before_decay, before_sum = prefix_2((own_decay, sketch), "tm", combine, identity)
    prefix = (
        own_decay[None, :] * before_sum + sketch + (before_decay * own_decay)[None, :] * prior_rows
    )
    padded = with_halo(prefix[None], (("bin", 0),), 1)
    mixed = padded[1] + 0.25 * (padded[0] + padded[2])
    local_gram = lax.dot_general(
        mixed,
        mixed,
        (((0,), (0,)), ((), ())),
        precision=lax.Precision.HIGHEST,
        preferred_element_type=jnp.float32,
    )
    gram = lax.psum(local_gram, "rx")
    factor = jnp.linalg.cholesky(gram)
    ortho = jax.scipy.linalg.solve_triangular(factor, mixed.T, lower=True).T
    local_coords = jnp.dot(
        block_data.astype(jnp.float32),
        ortho,
        precision=lax.Precision.HIGHEST,
        preferred_element_type=jnp.float32,
    )
    coords = lax.psum(local_coords.astype(jnp.bfloat16), "rx").astype(jnp.float32)
    receivers = rows * lax.axis_size("rx")
    basis = (math.sqrt(receivers) * ortho).astype(jnp.bfloat16)
    return (basis[None, None], coords[None])


def solution(mesh):
    return jax.shard_map(
        body,
        mesh=mesh,
        in_specs=(
            P("bin", "tm", "rx"),
            P("bin", "tm", None),
            P("bin", "tm", None),
            P("bin", "rx", None),
        ),
        out_specs=(P("bin", "tm", "rx", None), P("bin", "tm", None)),
        check_vma=False,
    )
```

profile of v0, /device:TPU:2, one launch (start us, length us, event | category | flops | bytes accessed | tf_op | source)
XLA Modules:
  0.0 489.7 jit_solution(11235781154400756800)
XLA Ops:
  8.1 2.3 fusion.15
  10.5 23.6 %all-gather = f32[16,1,512]{2,1,0:T(1,128)S(1)} all-gather(f32[1,1,512]{2,1,0:T(1,128)} %param.8), channel_id=2, replica_groups=mesh['rx'=8,'tm'=16,'bin'=4] {'tm'}, dimensions={0}, use_global_device_ids=true | all-gather | bytes 34816 | tf_op jit(solution)/shard_map/all_gather | solution.py:10
  34.1 79.9 %all-gather.4.cloned.1.call-done = f32[8192,512]{1,0:T(8,128)} async-done(((f32[512,512]{1,0:T(8,128)}), f32[8192,512]{1,0:T(8,128)}) %all-gather.4.cloned.1.call-update) | async-done | bytes 16777232 | tf_op jit(solution)/shard_map/all_gather | solution.py:10
  114.5 3.4 collective-permute-start
  117.9 2.5 collective-permute-start.1
  120.4 21.0 %collective-permute-done = f32[1,512,512]{2,1,0:T(8,128)S(1)} collective-permute-done((f32[1,512,512]{2,1,0:T(8,128)S(1)}, f32[1,512,512]{2,1,0:T(8,128)S(1)}, u32[]{:S(2)}, u32[]{:S(2)}) %collective-permute-start) | collective-permute-done | bytes 1048608 | tf_op jit(solution)/shard_map/ppermute | solution.py:26
  141.4 3.7 collective-permute-done.1
  146.7 2.9 fusion.40
  150.1 101.0 %all-reduce.4.cloned.1.call-done = f32[512,512]{0,1:T(8,128)} async-done(((f32[512,512]{0,1:T(8,128)}), f32[512,512]{0,1:T(8,128)}) %all-reduce.4.cloned.1.call-update) | async-done | bytes 1048592 | tf_op jit(solution)/shard_map/psum | solution.py:66
  254.2 11.7 %cholesky.103 = f32[128,128]{1,0:T(8,128)S(1)} custom-call(f32[128,128]{1,0:T(8,128)S(1)} %cholesky.263), custom_call_target="Cholesky" | custom-call | tf_op jit(solution)/shard_map/jit(cholesky)/cholesky | solution.py:67
  266.0 9.8 %custom-call.31 = f32[1,128,128]{1,2,0:T(8,128)S(1)} custom-call(f32[1,128,128]{2,1,0:T(8,128)S(1)} %get-tuple-element.81), custom_call_target="InvertDiagBlocksLowerTriangular" | custom-call | tf_op jit(solution)/shard_map/jit(cholesky)/cholesky | solution.py:67
  277.2 11.7 %cholesky.215 = f32[128,128]{1,0:T(8,128)S(1)} custom-call(f32[128,128]{1,0:T(8,128)S(1)} %cholesky.267), custom_call_target="Cholesky" | custom-call | tf_op jit(solution)/shard_map/jit(cholesky)/cholesky | solution.py:67
  288.9 10.0 %custom-call.32 = f32[1,128,128]{1,2,0:T(8,128)S(1)} custom-call(f32[1,128,128]{2,1,0:T(8,128)S(1)} %get-tuple-element.78), custom_call_target="InvertDiagBlocksLowerTriangular" | custom-call | tf_op jit(solution)/shard_map/jit(cholesky)/cholesky | solution.py:67
  301.1 13.2 %cholesky.236 = f32[128,128]{1,0:T(8,128)} custom-call(f32[128,128]{1,0:T(8,128)} %cholesky.272), custom_call_target="Cholesky" | custom-call | tf_op jit(solution)/shard_map/jit(cholesky)/cholesky | solution.py:67
  316.4 11.3 %custom-call.33 = f32[1,128,128]{1,2,0:T(8,128)} custom-call(f32[1,128,128]{2,1,0:T(8,128)} %get-tuple-element.75), custom_call_target="InvertDiagBlocksLowerTriangular" | custom-call | tf_op jit(solution)/shard_map/jit(cholesky)/cholesky | solution.py:67
  329.1 11.7 %cholesky.253 = f32[128,128]{1,0:T(8,128)S(1)} custom-call(f32[128,128]{1,0:T(8,128)S(1)} %convolution_subtract_fusion.5), custom_call_target="Cholesky" | custom-call | tf_op jit(solution)/shard_map/jit(cholesky)/cholesky | solution.py:67
  345.1 10.9 %while.14 = (s32[]{:T(128)}, f32[512,512]{1,0:T(8,128)S(1)}, s32[4,2]{0,1:T(2,128)S(1)}, f32[4,128,128]{2,1,0:T(8,128)}, s32[]{:T(128)}) while((s32[]{:T(128)}, f32[512,512]{1,0:T(8,128)S(1)}, s32[4,2]{0,1:T(2,128)S(1)}, f32[4,128,128]{2,1,0:T(8,128)}, s32[]{:T(128)}) %tuple.49), condition=%wide.while_cond, body=%wide.while_body.sunk | while | flops 2 | bytes 132705 | solution.py:68
  345.8 2.1 bitcast_dynamic-update-slice_fusion.2
  348.5 2.1 bitcast_dynamic-update-slice_fusion.2
  351.2 2.1 bitcast_dynamic-update-slice_fusion.2
  354.0 2.1 bitcast_dynamic-update-slice_fusion.2
  356.0 40.1 %custom-call.34 = f32[4,128,128]{1,2,0:T(8,128)S(1)} custom-call(f32[4,128,128]{2,1,0:T(8,128)} %get-tuple-element.45), custom_call_target="InvertDiagBlocksLowerTriangular" | custom-call | tf_op jit(solution)/shard_map/jit(_solve_triangular)/triangular_solve | solution.py:68
  405.1 75.9 %all-reduce.6.cloned.1.call-done = bf16[1,256,512]{1,2,0:T(8,128)(2,1)} async-done(((bf16[1,256,512]{1,2,0:T(8,128)(2,1)}), bf16[1,256,512]{1,2,0:T(8,128)(2,1)}) %all-reduce.6.cloned.1.call-update) | async-done | bytes 262160 | tf_op jit(solution)/shard_map/psum | solution.py:75
  481.0 1.9 copy.14
  (66 shorter events, 27.1 us)
Async XLA Ops:
  7.2 1.0 copy-start
  7.2 107.0 %copy-start.5 = (f32[1,1,512]{2,1,0:T(1,128)S(1)}, f32[1,1,512]{2,1,0:T(1,128)}, u32[]{:S(2)}) copy-start(f32[1,1,512]{2,1,0:T(1,128)} %param.8) | copy-start | bytes 6148
  7.2 107.0 %copy-start.2 = (bf16[1,512,512]{2,1,0:T(8,128)(2,1)S(1)}, bf16[1,512,512]{2,1,0:T(8,128)(2,1)}, u32[]{:S(2)}) copy-start(bf16[1,512,512]{2,1,0:T(8,128)(2,1)} %param.9) | copy-start | bytes 1572868
  7.2 106.8 %all-gather.4.cloned.1.call-start = ((), (), s32[]{:S(2)}) async-start(), calls=%async_computation.2 | async-start | bytes 17825792 | tf_op jit(solution)/shard_map/all_gather | solution.py:10
  10.4 103.8 %copy-start.1 = (f32[512,512]{1,0:T(8,128)S(1)}, f32[512,512]{1,0:T(8,128)}, u32[]{:S(2)}) copy-start(f32[512,512]{1,0:T(8,128)} %fusion.15) | copy-start | bytes 3145732
  10.4 240.7 %all-reduce.4.cloned.1.call-start = ((), (), s32[]{:S(2)}) async-start(), calls=%async_computation | async-start | bytes 2097152 | tf_op jit(solution)/shard_map/psum | solution.py:66
  114.5 27.0 %collective-permute-start = (f32[1,512,512]{2,1,0:T(8,128)S(1)}, f32[1,512,512]{2,1,0:T(8,128)S(1)}, u32[]{:S(2)}, u32[]{:S(2)}) collective-permute-start(f32[1,512,512]{2,1,0:T(8,128)S(1)} %fusion.35), channel_id=1, source_target_pairs={{0,1},{1,2},{2,3},{4,5},{5,6},{6,7},{8,9},{9,10},{10,11},{12,13},{... | collective-permute-start | bytes 3145736 | tf_op jit(solution)/shard_map/ppermute | solution.py:26
  117.9 27.2 %collective-permute-start.1 = (f32[1,512,512]{2,1,0:T(8,128)S(1)}, f32[1,512,512]{2,1,0:T(8,128)S(1)}, u32[]{:S(2)}, u32[]{:S(2)}) collective-permute-start(f32[1,512,512]{2,1,0:T(8,128)S(1)} %fusion.35), channel_id=1, source_target_pairs={{1,0},{2,1},{3,2},{5,4},{6,5},{7,6},{9,8},{10,9},{11,10},{13,12},{... | collective-permute-start | bytes 3145736 | tf_op jit(solution)/shard_map/ppermute | solution.py:29
  149.6 331.4 %all-reduce.6.cloned.1.call-start = ((), (), s32[]{:S(2)}) async-start(), calls=%async_computation.1 | async-start | bytes 524288 | tf_op jit(solution)/shard_map/psum | solution.py:75
  276.5 0.7 copy-start.3
  396.1 1.1 copy-start.4
Sparse Core Ops, SparseCore 0:
  10.5 103.3 all-gather.3
  149.7 101.3 all-reduce.3
  404.1 76.8 all-reduce.5
where the time goes:
time: 495 us; the launch traced here: 490 us
  waiting for transfers between devices  282 us (57%)
  other arithmetic  127 us (26%)
  blocking collectives  23.6 us (5%)
  local copies, waits for them, and re-layouts  17.8 us (4%)
  between operations  16.8 us (3%)
  matrix products  16.5 us (3%)
  starting transfers between devices  6.49 us (1%)
    psum x1, waiting for transfers between devices, body(): gram = lax.psum(local_gram, 'rx')  101 us
    another operation x14, other arithmetic, body(): factor = jnp.linalg.cholesky(gram)  82.9 us
    all_gather x1, waiting for transfers between devices, prefix_2(): gathered = jax.tree.map(lambda a: lax.all_gather(a, axis), part)  79.9 us
    psum x1, waiting for transfers between devices, body(): lax.psum(local_coords.astype(jnp.bfloat16), 'rx').astype(jnp.float32)  75.9 us
    another operation x3, other arithmetic, body(): ortho = jax.scipy.linalg.solve_triangular(factor, mixed.T, lower=True).T  40.4 us
    all_gather x1, blocking collectives, prefix_2(): gathered = jax.tree.map(lambda a: lax.all_gather(a, axis), part)  23.6 us
    ppermute x1, waiting for transfers between devices, with_halo(): lax.ppermute(lax.slice_in_dim(block, block.shape[dim] - width, None, axis...  21 us
    another operation x12, local copies, waits for them, and re-layouts  10.9 us
  transfers between devices with their start and end apart: 5, of which 5 were waited for; matrix products, arithmetic and copies ran while one was open for 0% of the time, Pallas kernels for 0%

commit v1 on v0

--- a/solution.py
+++ b/solution.py
@@ -3,6 +3,11 @@
 import jax.numpy as jnp
 from jax import lax
 from jax.sharding import PartitionSpec as P
+
+
+def change_regions(sheet, link_axis="rx"):
+    found_now = jnp.sum(lax.all_gather(sheet, axis_name=link_axis), axis=0)
+    return found_now
 
 
 def prefix_2(part, axis, combine, identity):
@@ -72,7 +77,7 @@
         precision=lax.Precision.HIGHEST,
         preferred_element_type=jnp.float32,
     )
-    coords = lax.psum(local_coords.astype(jnp.bfloat16), "rx").astype(jnp.float32)
+    coords = change_regions(local_coords.astype(jnp.bfloat16)).astype(jnp.float32)
     receivers = rows * lax.axis_size("rx")
     basis = (math.sqrt(receivers) * ortho).astype(jnp.bfloat16)
     return (basis[None, None], coords[None])

time: 495 us -> 464 us (0.937)
  waiting for transfers between devices: 282 us -> 253 us
  other arithmetic: 127 us -> 122 us
    psum x1 -> x0, waiting for transfers between devices: 75.9 us -> none  [body(): lax.psum(local_coords.astype(jnp.bfloat16), 'rx').astype(jnp.float32)]
    all_gather x0 -> x1, waiting for transfers between devices: none -> 47.9 us  [change_regions(): found_now = jnp.sum(lax.all_gather(sheet, axis_name=link_axis), axis=0)]
where the time goes in v1:
time: 464 us; the launch traced here: 460 us
  waiting for transfers between devices  253 us (55%)
  other arithmetic  122 us (26%)
  blocking collectives  23.2 us (5%)
  local copies, waits for them, and re-layouts  19.9 us (4%)
  matrix products  18.4 us (4%)
  between operations  16.9 us (4%)
  starting transfers between devices  6.49 us (1%)
    psum x1, waiting for transfers between devices, body(): gram = lax.psum(local_gram, 'rx')  99.6 us
    all_gather x1, waiting for transfers between devices, prefix_2(): gathered = jax.tree.map(lambda a: lax.all_gather(a, axis), part)  80.3 us
    another operation x14, other arithmetic, body(): factor = jnp.linalg.cholesky(gram)  78.7 us
    all_gather x1, waiting for transfers between devices, change_regions(): found_now = jnp.sum(lax.all_gather(sheet, axis_name=link_axis), axis=0)  47.9 us
    another operation x3, other arithmetic, body(): ortho = jax.scipy.linalg.solve_triangular(factor, mixed.T, lower=True).T  40.4 us
    all_gather x1, blocking collectives, prefix_2(): gathered = jax.tree.map(lambda a: lax.all_gather(a, axis), part)  23.2 us
    ppermute x1, waiting for transfers between devices, with_halo(): lax.ppermute(lax.slice_in_dim(block, block.shape[dim] - width, None, axis...  21.8 us
    another operation x12, local copies, waits for them, and re-layouts  10.6 us
  transfers between devices with their start and end apart: 5, of which 5 were waited for; matrix products, arithmetic and copies ran while one was open for 0% of the time, Pallas kernels for 0%

profile of v1, /device:TPU:2, one launch (start us, length us, event | category | flops | bytes accessed | tf_op | source)
XLA Modules:
  0.0 459.6 jit_solution(7548295647289480427)
XLA Ops:
  8.1 2.3 fusion.15
  10.5 23.2 %all-gather = f32[16,1,512]{2,1,0:T(1,128)S(1)} all-gather(f32[1,1,512]{2,1,0:T(1,128)S(1)} %copy-done.7), channel_id=2, replica_groups=mesh['rx'=8,'tm'=16,'bin'=4] {'tm'}, dimensions={0}, use_global_device_ids=true | all-gather | bytes 34816 | tf_op jit(solution)/shard_map/all_gather | solution.py:15
  33.7 80.3 %all-gather.6.cloned.1.call-done = f32[8192,512]{1,0:T(8,128)} async-done(((f32[512,512]{1,0:T(8,128)}), f32[8192,512]{1,0:T(8,128)}) %all-gather.6.cloned.1.call-update) | async-done | bytes 16777232 | tf_op jit(solution)/shard_map/all_gather | solution.py:15
  115.8 3.4 collective-permute-start
  119.1 2.5 collective-permute-start.1
  121.7 21.8 %collective-permute-done = f32[1,512,512]{2,1,0:T(8,128)S(1)} collective-permute-done((f32[1,512,512]{2,1,0:T(8,128)S(1)}, f32[1,512,512]{2,1,0:T(8,128)S(1)}, u32[]{:S(2)}, u32[]{:S(2)}) %collective-permute-start) | collective-permute-done | bytes 1048608 | tf_op jit(solution)/shard_map/ppermute | solution.py:31
  143.5 3.1 collective-permute-done.1
  147.2 2.9 fusion.40
  150.6 99.6 %all-reduce.3.cloned.1.call-done = f32[512,512]{0,1:T(8,128)} async-done(((f32[512,512]{0,1:T(8,128)}), f32[512,512]{0,1:T(8,128)}) %all-reduce.3.cloned.1.call-update) | async-done | bytes 1048592 | tf_op jit(solution)/shard_map/psum | solution.py:71
  253.1 11.7 %cholesky.103 = f32[128,128]{1,0:T(8,128)S(1)} custom-call(f32[128,128]{1,0:T(8,128)S(1)} %cholesky.263), custom_call_target="Cholesky" | custom-call | tf_op jit(solution)/shard_map/jit(cholesky)/cholesky | solution.py:72
  265.0 9.8 %custom-call.31 = f32[1,128,128]{1,2,0:T(8,128)S(1)} custom-call(f32[1,128,128]{2,1,0:T(8,128)S(1)} %get-tuple-element.81), custom_call_target="InvertDiagBlocksLowerTriangular" | custom-call | tf_op jit(solution)/shard_map/jit(cholesky)/cholesky | solution.py:72
  277.3 11.7 %cholesky.215 = f32[128,128]{1,0:T(8,128)S(1)} custom-call(f32[128,128]{1,0:T(8,128)S(1)} %cholesky.267), custom_call_target="Cholesky" | custom-call | tf_op jit(solution)/shard_map/jit(cholesky)/cholesky | solution.py:72
  289.0 10.0 %custom-call.32 = f32[1,128,128]{1,2,0:T(8,128)S(1)} custom-call(f32[1,128,128]{2,1,0:T(8,128)S(1)} %get-tuple-element.78), custom_call_target="InvertDiagBlocksLowerTriangular" | custom-call | tf_op jit(solution)/shard_map/jit(cholesky)/cholesky | solution.py:72
  300.6 11.7 %cholesky.236 = f32[128,128]{1,0:T(8,128)S(1)} custom-call(f32[128,128]{1,0:T(8,128)S(1)} %cholesky.272), custom_call_target="Cholesky" | custom-call | tf_op jit(solution)/shard_map/jit(cholesky)/cholesky | solution.py:72
  313.1 9.8 %custom-call.33 = f32[1,128,128]{1,2,0:T(8,128)S(1)} custom-call(f32[1,128,128]{2,1,0:T(8,128)S(1)} %get-tuple-element.75), custom_call_target="InvertDiagBlocksLowerTriangular" | custom-call | tf_op jit(solution)/shard_map/jit(cholesky)/cholesky | solution.py:72
  324.3 11.7 %cholesky.253 = f32[128,128]{1,0:T(8,128)S(1)} custom-call(f32[128,128]{1,0:T(8,128)S(1)} %convolution_subtract_fusion.5), custom_call_target="Cholesky" | custom-call | tf_op jit(solution)/shard_map/jit(cholesky)/cholesky | solution.py:72
  340.4 10.6 %while.14 = (s32[]{:T(128)}, f32[512,512]{1,0:T(8,128)S(1)}, s32[4,2]{0,1:T(2,128)S(1)}, f32[4,128,128]{2,1,0:T(8,128)}, s32[]{:T(128)}) while((s32[]{:T(128)}, f32[512,512]{1,0:T(8,128)S(1)}, s32[4,2]{0,1:T(2,128)S(1)}, f32[4,128,128]{2,1,0:T(8,128)}, s32[]{:T(128)}) %tuple.49), condition=%wide.while_cond, body=%wide.while_body.sunk | while | flops 2 | bytes 132705 | solution.py:73
  341.0 2.0 bitcast_dynamic-update-slice_fusion.2
  343.7 2.0 bitcast_dynamic-update-slice_fusion.2
  346.3 2.0 bitcast_dynamic-update-slice_fusion.2
  349.0 2.0 bitcast_dynamic-update-slice_fusion.2
  351.0 40.1 %custom-call.34 = f32[4,128,128]{1,2,0:T(8,128)S(1)} custom-call(f32[4,128,128]{2,1,0:T(8,128)} %get-tuple-element.45), custom_call_target="InvertDiagBlocksLowerTriangular" | custom-call | tf_op jit(solution)/shard_map/jit(_solve_triangular)/triangular_solve | solution.py:73
  400.1 47.9 %all-gather.8.cloned.1.call-done = bf16[2048,512]{0,1:T(8,128)(2,1)} async-done(((bf16[256,512]{0,1:T(8,128)(2,1)}), bf16[2048,512]{0,1:T(8,128)(2,1)}) %all-gather.8.cloned.1.call-update) | async-done | bytes 2097168 | tf_op jit(solution)/shard_map/all_gather | solution.py:9
  448.0 2.3 copy.16
  (73 shorter events, 29.0 us)
Async XLA Ops:
  7.2 1.0 copy-start
  7.2 3.3 copy-start.7
  7.2 106.8 %all-gather.6.cloned.1.call-start = ((), (), s32[]{:S(2)}) async-start(), calls=%async_computation.1 | async-start | bytes 17825792 | tf_op jit(solution)/shard_map/all_gather | solution.py:15
  10.4 239.8 %all-reduce.3.cloned.1.call-start = ((), (), s32[]{:S(2)}) async-start(), calls=%async_computation | async-start | bytes 2097152 | tf_op jit(solution)/shard_map/psum | solution.py:71
  114.1 1.2 copy-start.1
  114.1 1.3 copy-start.4
  114.2 32.5 %copy-start.5 = (bf16[1,512,512]{2,1,0:T(8,128)(2,1)S(1)}, bf16[1,512,512]{2,1,0:T(8,128)(2,1)}, u32[]{:S(2)}) copy-start(bf16[1,512,512]{2,1,0:T(8,128)(2,1)} %param.9) | copy-start | bytes 1572868
  115.8 27.7 %collective-permute-start = (f32[1,512,512]{2,1,0:T(8,128)S(1)}, f32[1,512,512]{2,1,0:T(8,128)S(1)}, u32[]{:S(2)}, u32[]{:S(2)}) collective-permute-start(f32[1,512,512]{2,1,0:T(8,128)S(1)} %fusion.35), channel_id=1, source_target_pairs={{0,1},{1,2},{2,3},{4,5},{5,6},{6,7},{8,9},{9,10},{10,11},{12,13},{... | collective-permute-start | bytes 3145736 | tf_op jit(solution)/shard_map/ppermute | solution.py:31
  119.1 27.5 %collective-permute-start.1 = (f32[1,512,512]{2,1,0:T(8,128)S(1)}, f32[1,512,512]{2,1,0:T(8,128)S(1)}, u32[]{:S(2)}, u32[]{:S(2)}) collective-permute-start(f32[1,512,512]{2,1,0:T(8,128)S(1)} %fusion.35), channel_id=1, source_target_pairs={{1,0},{2,1},{3,2},{5,4},{6,5},{7,6},{9,8},{10,9},{11,10},{13,12},{... | collective-permute-start | bytes 3145736 | tf_op jit(solution)/shard_map/ppermute | solution.py:34
  150.1 297.9 %all-gather.8.cloned.1.call-start = ((), (), s32[]{:S(2)}) async-start(), calls=%async_computation.2 | async-start | bytes 2359296 | tf_op jit(solution)/shard_map/all_gather | solution.py:9
  250.2 1.7 copy-start.2
  252.1 1.0 copy-start.3
  391.1 1.1 copy-start.6
Sparse Core Ops, SparseCore 0:
  10.5 103.3 all-gather.5
  150.2 99.9 all-reduce.2
  399.1 48.8 all-gather.7
